TPU v7x, 256 devices: a whole 4x4x8 slice. The times are simulated.
256 devices in a mesh: blk: 4 (over x), shard: 64 (over y, z, core).
Axes of the slice: x: 4, y: 4, z: 8, core: 2. Of those that a mesh axis runs over, the one named last changes fastest.
Arguments:
- table: bfloat16 [524288, 400], P(('blk', 'shard')), may hold values from -3 to 3
- relation: bfloat16 [1345, 400], replicated, may hold values from -3 to 3
- owners: int32 [262144, 2], P(('blk', 'shard')), may hold values from 0 to 63, all different within a row; in each aligned block of 1024 rows (0 to 1023, 1024 to 2047, ...) at most 64 rows name the same one
- rows: int32 [262144, 2], P(('blk', 'shard')), may hold values from 0 to 2047
- rel_ids: int32 [262144], P(('blk', 'shard')), may hold values from 0 to 1344
- span_ids: int32 [256], P(('blk', 'shard')), may hold values from 0 to 1
Outputs:
- entity_grad: float32 [524288, 400], P(('blk', 'shard'))
- relation_grad: float32 [1345, 400], replicated
Inputs may be any that keep to these rules, and one draw needn't show every extreme that they name: Among the 1024 edges of one device no owner index is named by more than 64 edge ends; an edge's source and target owners differ; ends address rows of the devices with the same blk index.
All inputs are finite; a program needn't handle non-finite values.
Results may differ from a plain program's by a relative error of at most 0.0016.
Values may be sent and summed in bfloat16 or wider, within the bound.
No kernel may reach another device: no remote copies, remote signals or barrier semaphores. Data moves between devices by JAX's collectives and lax.ppermute only.
A program may use at most 128 MiB of HBM per device.

v0:
```python
import math
import jax
import jax.numpy as jnp
from jax import lax
from jax.sharding import PartitionSpec as P

NEG = 1024


def spread(value, axis, n):
    copies = jnp.broadcast_to(value[None], (n,) + value.shape)
    return lax.all_to_all(copies, axis, 0, 0, tiled=False)


def owner_rank(flat_owner, n_shard):
    count = flat_owner.shape[0]
    onehot = flat_owner[:, None] == jnp.arange(n_shard, dtype=jnp.int32)[None, :]
    index = jnp.arange(count, dtype=jnp.int32)
    earlier = (index[:, None] > index[None, :]).astype(jnp.bfloat16)
    before = jnp.dot(earlier, onehot.astype(jnp.bfloat16), preferred_element_type=jnp.float32)
    return jnp.sum(jnp.where(onehot, before, 0.0), axis=1).astype(jnp.int32)


def reduce_relation(local_relation):
    return lax.psum(local_relation, ("blk", "shard"))


def shards(table, relation, owners, rows, rel_ids, span_ids):
    n_shard = lax.axis_size("shard")
    n_blk = lax.axis_size("blk")
    edges = owners.shape[0]
    rows_own = table.shape[0]
    width = table.shape[1]
    half = width // 2
    capacity = 4 * edges // n_shard
    negatives = NEG
    span_start = span_ids[0] * negatives
    span = lax.dynamic_slice_in_dim(table, span_start, negatives, 0)
    spans = spread(span, "blk", n_blk).reshape(n_blk * negatives, width)
    flat_owner = owners.reshape(-1)
    flat_row = rows.reshape(-1)
    ranking = owner_rank(flat_owner, n_shard)
    slots = flat_owner * capacity + ranking
    requests = (
        jnp.zeros((n_shard * capacity,), jnp.int32)
        .at[slots]
        .set(flat_row)
        .reshape(n_shard, capacity)
    )
    asked_rows = lax.all_to_all(requests, "shard", split_axis=0, concat_axis=0, tiled=True)
    fetched = lax.all_to_all(table[asked_rows], "shard", split_axis=0, concat_axis=0, tiled=True)
    gotten = fetched.reshape(n_shard * capacity, width)[slots].reshape(edges, 2, width)
    source = gotten[:, 0].astype(jnp.float32)
    target = gotten[:, 1].astype(jnp.float32)
    rel_rows = relation[rel_ids].astype(jnp.float32)
    s_re, s_im = (source[:, :half], source[:, half:])
    r_re, r_im = (rel_rows[:, :half], rel_rows[:, half:])
    query = jnp.concatenate([s_re * r_re - s_im * r_im, s_re * r_im + s_im * r_re], axis=1)
    pos_grad = jax.nn.sigmoid(jnp.sum(query * target, axis=1)) - 1.0
    query_bf = query.astype(jnp.bfloat16)
    weight = 1.0 / math.sqrt(n_blk * negatives)
    neg_score = lax.dot_general(
        query_bf, spans, (((1,), (1,)), ((), ())), preferred_element_type=jnp.float32
    )
    neg_grad = (weight * jax.nn.sigmoid(neg_score)).astype(jnp.bfloat16)
    query_grad = pos_grad[:, None] * target + jnp.dot(
        neg_grad, spans, preferred_element_type=jnp.float32
    )
    span_part = lax.dot_general(
        neg_grad, query_bf, (((0,), (0,)), ((), ())), preferred_element_type=jnp.float32
    )
    carried = lax.all_to_all(
        span_part.reshape(n_blk, negatives, width), "blk", 0, 0, tiled=False
    ).sum(axis=0)
    q_re, q_im = (query_grad[:, :half], query_grad[:, half:])
    source_grad = jnp.concatenate([q_re * r_re + q_im * r_im, q_im * r_re - q_re * r_im], axis=1)
    rel_term = jnp.concatenate([q_re * s_re + q_im * s_im, q_im * s_re - q_re * s_im], axis=1)
    target_grad = pos_grad[:, None] * query
    local_relation = jnp.zeros((relation.shape[0], width), jnp.float32).at[rel_ids].add(rel_term)
    relation_grad = reduce_relation(local_relation)
    end_grads = jnp.stack([source_grad, target_grad], axis=1).reshape(2 * edges, width)
    outgoing = jnp.zeros((n_shard * capacity, width), jnp.float32).at[slots].set(end_grads)
    arrived = lax.all_to_all(
        outgoing.reshape(n_shard, capacity, width), "shard", split_axis=0, concat_axis=0, tiled=True
    )
    entity_grad = (
        jnp.zeros((rows_own, width), jnp.float32)
        .at[asked_rows.reshape(-1)]
        .add(arrived.reshape(-1, width))
    )
    current = lax.dynamic_slice_in_dim(entity_grad, span_start, negatives, 0)
    entity_grad = lax.dynamic_update_slice_in_dim(entity_grad, current + carried, span_start, 0)
    return (entity_grad, relation_grad)


def solution(mesh):
    in_specs = (
        P(("blk", "shard"), None),
        P(),
        P(("blk", "shard"), None),
        P(("blk", "shard"), None),
        P(("blk", "shard")),
        P(("blk", "shard")),
    )
    out_specs = (P(("blk", "shard"), None), P())
    return jax.shard_map(shards, mesh=mesh, in_specs=in_specs, out_specs=out_specs, check_vma=False)
```

profile of v0, /device:TPU:16, one launch (start us, length us, event | category | flops | bytes accessed | tf_op | source)
XLA Modules:
  0.0 695.9 jit_solution(672101288420316935)
XLA Ops:
  12.5 8.1 %scatter_custom_fusion = s32[4096]{0:T(1024)S(1)} fusion(s32[2048]{0:T(1024)S(1)} %bitcast.43, s32[2048]{0:T(1024)S(1)} %reshape.226, s32[]{:T(128)} %constant.11.clone.1), kind=kCustom, calls=%fused_computation.45 | custom fusion | bytes 16388 | tf_op jit(solution)/shard_map/scatter | solution.py:47
  21.3 12.1 %all-to-all-start = ((s32[64,1,64]{2,1,0:T(1,128)}), s32[64,1,64]{2,1,0:T(1,128)S(1)}, u32[]{:S(2)}, u32[]{:S(2)}) async-start(s32[64,1,64]{2,1,0:T(1,128)} %all_to_all.20), calls=%async_computation | async-start | bytes 65536 | tf_op jit(solution)/shard_map/all_to_all | solution.py:50
  34.1 6.9 all-to-all-done
  43.1 4.7 all-to-all-start.2
  50.7 17.4 %gather_fusion = bf16[4096,400]{1,0:T(8,128)(2,1)} fusion(bf16[2048,400]{1,0:T(8,128)(2,1)S(1)} %copy.43, s32[4096]{0:T(1024)S(1)} %broadcast_clamp_fusion), kind=kCustom, calls=%fused_computation | custom fusion | bytes 6569984 | tf_op jit(solution)/shard_map/gather | solution.py:51
  68.1 19.1 %all-to-all-done.2 = bf16[4,1024,400]{1,2,0:T(8,128)(2,1)} async-done(((bf16[4,1024,400]{1,2,0:T(8,128)(2,1)}), bf16[4,1024,400]{1,2,0:T(8,128)(2,1)}, u32[]{:S(2)}, u32[]{:S(2)}) %all-to-all-start.2) | async-done | bytes 3276832 | tf_op jit(solution)/shard_map/all_to_all | solution.py:12
  87.2 8.2 %all-to-all-start.1 = ((bf16[64,64,400]{2,1,0:T(8,128)(2,1)}), bf16[64,64,400]{2,1,0:T(8,128)(2,1)}, u32[]{:S(2)}, u32[]{:S(2)}) async-start(bf16[64,64,400]{2,1,0:T(8,128)(2,1)} %bitcast.36), calls=%async_computation.1 | async-start | bytes 8388608 | tf_op jit(solution)/shard_map/all_to_all | solution.py:51
  96.3 4.0 gather_fusion.2
  102.2 4.1 copy.60
  106.3 81.8 %all-to-all-done.1 = bf16[64,64,400]{2,1,0:T(8,128)(2,1)} async-done(((bf16[64,64,400]{2,1,0:T(8,128)(2,1)}), bf16[64,64,400]{2,1,0:T(8,128)(2,1)}, u32[]{:S(2)}, u32[]{:S(2)}) %all-to-all-start.1) | async-done | bytes 3276832 | tf_op jit(solution)/shard_map/all_to_all | solution.py:51
  188.1 12.0 %gather_fusion.1 = bf16[2048,400]{1,0:T(8,128)(2,1)} fusion(bf16[4096,400]{1,0:T(8,128)(2,1)} %bitcast.5, s32[2048]{0:T(1024)S(1)} %broadcast_clamp_fusion.1), kind=kCustom, calls=%fused_computation.1 | custom fusion | bytes 3284992 | tf_op jit(solution)/shard_map/gather | solution.py:52
  200.1 2.8 reshape.190
  202.9 4.2 fusion.20
  207.1 6.0 copy.57
  216.9 7.5 %multiply_convert_fusion = bf16[1024,4096]{1,0:T(8,128)(2,1)S(1)} fusion(bf16[4096,400]{0,1:T(8,128)(2,1)S(1)} %bitcast.41, f32[1024,200]{0,1:T(8,128)S(1)} %get-tuple-element.13, f32[1024,200]{0,1:T(8,128)S(1)} %get-tuple-element.12), kind=kOutput, calls=%fused_computation.7 | convolution fusion | flops 3378053120 | bytes 13303808 | tf_op jit(solution)/shard_map/dot_general | solution.py:62
  224.4 3.6 fusion.13
  228.1 3.6 copy.62
  231.7 5.5 all-to-all-start.4
  237.2 5.8 copy.58
  244.9 8.1 %fusion.7 = f32[1024,400]{0,1:T(8,128)S(1)} fusion(bf16[1024,4096]{1,0:T(8,128)(2,1)} %copy-done.11, bf16[4096,400]{0,1:T(8,128)(2,1)} %bitcast.40, bf16[1024,1,400]{0,2,1:T(8,128)(2,1)} %copy.58, f32[1024]{0:T(1024)S(1)} %divide_add_fusion), kind=kOutput, calls=%fused_computation.21 | convolution fusion | flops 3356672000 | bytes 14127104 | tf_op jit(solution)/shard_map/dot_general | solution.py:66
  256.8 4.5 copy.49
  261.4 6.2 reshape.234
  267.5 13.4 %scatter_custom_fusion.1 = f32[4096,400]{1,0:T(8,128)} fusion(s32[2048]{0:T(1024)S(1)} %bitcast.45, f32[2048,400]{1,0:T(8,128)} %reshape.234, f32[]{:T(128)} %constant.10.clone.1), kind=kCustom, calls=%fused_computation.11 | custom fusion | bytes 6554112 | tf_op jit(solution)/shard_map/scatter | solution.py:82
  280.9 29.8 %all-to-all-done.4 = f32[4,1024,400]{1,2,0:T(8,128)} async-done(((f32[4,1024,400]{1,2,0:T(8,128)}), f32[4,1024,400]{1,2,0:T(8,128)}, u32[]{:S(2)}, u32[]{:S(2)}) %all-to-all-start.4) | async-done | bytes 6553632 | tf_op jit(solution)/shard_map/all_to_all | solution.py:72
  310.7 9.9 %all-to-all-start.3 = ((f32[64,64,400]{2,1,0:T(8,128)}), f32[64,64,400]{2,1,0:T(8,128)}, u32[]{:S(2)}, u32[]{:S(2)}) async-start(f32[64,64,400]{2,1,0:T(8,128)} %bitcast.34), calls=%async_computation.3 | async-start | bytes 16777216 | tf_op jit(solution)/shard_map/all_to_all | solution.py:83
  322.8 8.9 %scatter_custom_fusion.3 = f32[1345,400]{1,0:T(8,128)} fusion(s32[1024]{0:T(1024)S(1)} %get-tuple-element.18, f32[1024,400]{1,0:T(8,128)} %copy.53, f32[]{:T(128)} %constant.10.clone.1), kind=kCustom, calls=%fused_computation.26 | custom fusion | flops 409600 | bytes 2152512 | tf_op jit(solution)/shard_map/scatter-add | solution.py:79
  333.1 307.1 %all-reduce.2.cloned.1.call-done = f32[1345,400]{1,0:T(8,128)} async-done(((f32[1345,400]{1,0:T(8,128)}), f32[1345,400]{1,0:T(8,128)}) %all-reduce.2.cloned.1.call-update) | async-done | bytes 2152016 | tf_op jit(solution)/shard_map/psum | solution.py:25
  640.2 3.3 copy.55
  643.5 4.9 reduce_sum.29
  650.3 30.0 %scatter_custom_fusion.2 = f32[2048,400]{1,0:T(8,128)} fusion(s32[4096]{0:T(1024)S(1)} %bitcast.47, f32[4096,400]{1,0:T(8,128)} %bitcast.14, f32[]{:T(128)} %constant.10.clone.1), kind=kCustom, calls=%fused_computation.16 | custom fusion | flops 1638400 | bytes 3277312 | tf_op jit(solution)/shard_map/scatter-add | solution.py:89
  680.3 3.4 add_dynamic-update-slice_fusion
  683.7 5.2 copy.54
  (64 shorter events, 28.9 us)
Async XLA Ops:
  10.8 23.2 %copy-start.5 = (bf16[2048,400]{0,1:T(8,128)(2,1)S(1)}, bf16[2048,400]{0,1:T(8,128)(2,1)}, u32[]{:S(2)}) copy-start(bf16[2048,400]{0,1:T(8,128)(2,1)} %param.6) | copy-start | bytes 4915204
  21.3 19.7 %all-to-all-start = ((s32[64,1,64]{2,1,0:T(1,128)}), s32[64,1,64]{2,1,0:T(1,128)S(1)}, u32[]{:S(2)}, u32[]{:S(2)}) async-start(s32[64,1,64]{2,1,0:T(1,128)} %all_to_all.20), calls=%async_computation | async-start | bytes 65536 | tf_op jit(solution)/shard_map/all_to_all | solution.py:50
  43.1 44.1 %all-to-all-start.2 = ((bf16[4,1024,400]{1,2,0:T(8,128)(2,1)}), bf16[4,1024,400]{1,2,0:T(8,128)(2,1)}, u32[]{:S(2)}, u32[]{:S(2)}) async-start(bf16[4,1024,400]{1,2,0:T(8,128)(2,1)} %broadcast_in_dim.18), calls=%async_computation.2 | async-start | bytes 6553600 | tf_op jit(solution)/shard_map/all_to_all | solution.py:12
  87.2 8.2 %copy-start.9 = (bf16[1345,400]{0,1:T(8,128)(2,1)S(1)}, bf16[1345,400]{0,1:T(8,128)(2,1)}, u32[]{:S(2)}) copy-start(bf16[1345,400]{0,1:T(8,128)(2,1)} %param.7) | copy-start | bytes 3228004
  87.2 9.1 %copy-start.10 = (s32[1024]{0:T(1024)S(1)}, s32[1024]{0:T(1024)}, u32[]{:S(2)}) copy-start(s32[1024]{0:T(1024)} %param.10) | copy-start | bytes 12292
  87.2 100.9 %all-to-all-start.1 = ((bf16[64,64,400]{2,1,0:T(8,128)(2,1)}), bf16[64,64,400]{2,1,0:T(8,128)(2,1)}, u32[]{:S(2)}, u32[]{:S(2)}) async-start(bf16[64,64,400]{2,1,0:T(8,128)(2,1)} %bitcast.36), calls=%async_computation.1 | async-start | bytes 8388608 | tf_op jit(solution)/shard_map/all_to_all | solution.py:51
  207.1 7.3 %copy-start = (f32[1024,400]{0,1:T(8,128)S(1)}, f32[1024,400]{0,1:T(8,128)}, u32[]{:S(2)}) copy-start(f32[1024,400]{0,1:T(8,128)} %convert_element_type.40) | copy-start | bytes 4915204
  214.4 2.5 copy-start.6
  214.7 9.7 %copy-start.1 = (f32[1024,200]{0,1:T(8,128)}, f32[1024,200]{0,1:T(8,128)S(1)}, u32[]{:S(2)}) copy-start(f32[1024,200]{0,1:T(8,128)S(1)} %get-tuple-element.12) | copy-start | bytes 2457604
  214.7 9.7 %copy-start.3 = (f32[1024,200]{0,1:T(8,128)}, f32[1024,200]{0,1:T(8,128)S(1)}, u32[]{:S(2)}) copy-start(f32[1024,200]{0,1:T(8,128)S(1)} %get-tuple-element.13) | copy-start | bytes 2457604
  224.4 3.7 copy-start.11
  231.7 79.0 %all-to-all-start.4 = ((f32[4,1024,400]{1,2,0:T(8,128)}), f32[4,1024,400]{1,2,0:T(8,128)}, u32[]{:S(2)}, u32[]{:S(2)}) async-start(f32[4,1024,400]{1,2,0:T(8,128)} %bitcast.35), calls=%async_computation.4 | async-start | bytes 13107200 | tf_op jit(solution)/shard_map/all_to_all | solution.py:72
  254.9 1.1 copy-start.2
  254.9 1.4 copy-start.4
  310.7 10.2 %copy-start.7 = (f32[1024,200]{0,1:T(8,128)S(1)}, f32[1024,200]{0,1:T(8,128)}, u32[]{:S(2)}) copy-start(f32[1024,200]{0,1:T(8,128)} %get-tuple-element.8) | copy-start | bytes 2457604
  310.7 10.2 %copy-start.8 = (f32[1024,200]{0,1:T(8,128)S(1)}, f32[1024,200]{0,1:T(8,128)}, u32[]{:S(2)}) copy-start(f32[1024,200]{0,1:T(8,128)} %get-tuple-element.9) | copy-start | bytes 2457604
  310.7 339.6 %all-to-all-start.3 = ((f32[64,64,400]{2,1,0:T(8,128)}), f32[64,64,400]{2,1,0:T(8,128)}, u32[]{:S(2)}, u32[]{:S(2)}) async-start(f32[64,64,400]{2,1,0:T(8,128)} %bitcast.34), calls=%async_computation.3 | async-start | bytes 16777216 | tf_op jit(solution)/shard_map/all_to_all | solution.py:83
  320.6 319.6 %all-reduce.2.cloned.1.call-start = ((), (), s32[]{:S(2)}) async-start(), calls=%async_computation.5 | async-start | bytes 5537792 | tf_op jit(solution)/shard_map/psum | solution.py:25
Sparse Core Ops, SparseCore 0:
  331.9 308.2 all-reduce.1
where the time goes:
time: 702 us; the launch traced here: 696 us
  waiting for transfers between devices  445 us (63%)
  local copies, waits for them, and re-layouts  118 us (17%)
  other arithmetic  56.5 us (8%)
  starting transfers between devices  40.6 us (6%)
  matrix products  20.9 us (3%)
  between operations  15.3 us (2%)
    psum x1, waiting for transfers between devices, reduce_relation(): return lax.psum(local_relation, ('blk', 'shard'))  307 us
    all_to_all x1, waiting for transfers between devices, shards(): lax.all_to_all(table[asked_rows], 'shard', split_axis=0, concat_axis=0, t...  81.8 us
    scatter-add x1, other arithmetic, shards(): entity_grad = jnp.zeros((rows_own, width), jnp.float32).at[asked_rows.res...  30 us
    all_to_all x1, waiting for transfers between devices, shards(): lax.all_to_all(span_part.reshape(n_blk, negatives, width), 'blk', 0, 0, t...  29.8 us
    unnamed x32, local copies, waits for them, and re-layouts  29.1 us
    all_to_all x1, waiting for transfers between devices, spread(): return lax.all_to_all(copies, axis, 0, 0, tiled=False)  19.1 us
    gather x1, local copies, waits for them, and re-layouts, shards(): table[asked_rows]  17.4 us
  transfers between devices with their start and end apart: 6, of which 5 were waited for; matrix products, arithmetic and copies ran while one was open for 14% of the time, Pallas kernels for 0%

commit v1 on v0

--- a/solution.py
+++ b/solution.py
@@ -22,7 +22,7 @@
 
 
 def reduce_relation(local_relation):
-    return lax.psum(local_relation, ("blk", "shard"))
+    return lax.psum(lax.psum(local_relation, "shard"), "blk")
 
 
 def shards(table, relation, owners, rows, rel_ids, span_ids):

time: 702 us -> 712 us (1.014)
  waiting for transfers between devices: 445 us -> 454 us
    psum x1 -> x2, waiting for transfers between devices: 307 us -> 316 us  [reduce_relation(): return lax.psum(lax.psum(local_relation, 'shard'), 'blk')]
  transfers between devices with their start and end apart: 6 -> 7, of which waited for: 5 -> 6; matrix products, arithmetic and copies ran while one was open for 14% -> 14% of each run, Pallas kernels for 0% -> 0%
where the time goes in v1:
time: 712 us; the launch traced here: 705 us
  waiting for transfers between devices  454 us (64%)
  local copies, waits for them, and re-layouts  118 us (17%)
  other arithmetic  56.5 us (8%)
  starting transfers between devices  40.6 us (6%)
  matrix products  20.9 us (3%)
  between operations  15.3 us (2%)
    psum x2, waiting for transfers between devices, reduce_relation(): return lax.psum(lax.psum(local_relation, 'shard'), 'blk')  316 us
    all_to_all x1, waiting for transfers between devices, shards(): lax.all_to_all(table[asked_rows], 'shard', split_axis=0, concat_axis=0, t...  81.8 us
    scatter-add x1, other arithmetic, shards(): entity_grad = jnp.zeros((rows_own, width), jnp.float32).at[asked_rows.res...  30 us
    all_to_all x1, waiting for transfers between devices, shards(): lax.all_to_all(span_part.reshape(n_blk, negatives, width), 'blk', 0, 0, t...  29.8 us
    unnamed x32, local copies, waits for them, and re-layouts  29.1 us
    all_to_all x1, waiting for transfers between devices, spread(): return lax.all_to_all(copies, axis, 0, 0, tiled=False)  19.1 us
    gather x1, local copies, waits for them, and re-layouts, shards(): table[asked_rows]  17.4 us
  transfers between devices with their start and end apart: 7, of which 6 were waited for; matrix products, arithmetic and copies ran while one was open for 14% of the time, Pallas kernels for 0%

profile of v1, /device:TPU:16, one launch (start us, length us, event | category | flops | bytes accessed | tf_op | source)
XLA Modules:
  0.0 705.3 jit_solution(10561702523959044197)
XLA Ops:
  12.5 8.1 %scatter_custom_fusion = s32[4096]{0:T(1024)S(1)} fusion(s32[2048]{0:T(1024)S(1)} %bitcast.43, s32[2048]{0:T(1024)S(1)} %reshape.226, s32[]{:T(128)} %constant.11.clone.1), kind=kCustom, calls=%fused_computation.45 | custom fusion | bytes 16388 | tf_op jit(solution)/shard_map/scatter | solution.py:47
  21.3 12.1 %all-to-all-start = ((s32[64,1,64]{2,1,0:T(1,128)}), s32[64,1,64]{2,1,0:T(1,128)S(1)}, u32[]{:S(2)}, u32[]{:S(2)}) async-start(s32[64,1,64]{2,1,0:T(1,128)} %all_to_all.20), calls=%async_computation | async-start | bytes 65536 | tf_op jit(solution)/shard_map/all_to_all | solution.py:50
  34.1 6.9 all-to-all-done
  43.1 4.7 all-to-all-start.2
  50.7 17.4 %gather_fusion = bf16[4096,400]{1,0:T(8,128)(2,1)} fusion(bf16[2048,400]{1,0:T(8,128)(2,1)S(1)} %copy.43, s32[4096]{0:T(1024)S(1)} %broadcast_clamp_fusion), kind=kCustom, calls=%fused_computation | custom fusion | bytes 6569984 | tf_op jit(solution)/shard_map/gather | solution.py:51
  68.1 19.1 %all-to-all-done.2 = bf16[4,1024,400]{1,2,0:T(8,128)(2,1)} async-done(((bf16[4,1024,400]{1,2,0:T(8,128)(2,1)}), bf16[4,1024,400]{1,2,0:T(8,128)(2,1)}, u32[]{:S(2)}, u32[]{:S(2)}) %all-to-all-start.2) | async-done | bytes 3276832 | tf_op jit(solution)/shard_map/all_to_all | solution.py:12
  87.2 8.2 %all-to-all-start.1 = ((bf16[64,64,400]{2,1,0:T(8,128)(2,1)}), bf16[64,64,400]{2,1,0:T(8,128)(2,1)}, u32[]{:S(2)}, u32[]{:S(2)}) async-start(bf16[64,64,400]{2,1,0:T(8,128)(2,1)} %bitcast.36), calls=%async_computation.1 | async-start | bytes 8388608 | tf_op jit(solution)/shard_map/all_to_all | solution.py:51
  96.3 4.0 gather_fusion.2
  102.2 4.1 copy.60
  106.3 81.8 %all-to-all-done.1 = bf16[64,64,400]{2,1,0:T(8,128)(2,1)} async-done(((bf16[64,64,400]{2,1,0:T(8,128)(2,1)}), bf16[64,64,400]{2,1,0:T(8,128)(2,1)}, u32[]{:S(2)}, u32[]{:S(2)}) %all-to-all-start.1) | async-done | bytes 3276832 | tf_op jit(solution)/shard_map/all_to_all | solution.py:51
  188.1 12.0 %gather_fusion.1 = bf16[2048,400]{1,0:T(8,128)(2,1)} fusion(bf16[4096,400]{1,0:T(8,128)(2,1)} %bitcast.5, s32[2048]{0:T(1024)S(1)} %broadcast_clamp_fusion.1), kind=kCustom, calls=%fused_computation.1 | custom fusion | bytes 3284992 | tf_op jit(solution)/shard_map/gather | solution.py:52
  202.9 4.2 fusion.20
  207.1 6.0 copy.57
  216.9 7.5 %multiply_convert_fusion = bf16[1024,4096]{1,0:T(8,128)(2,1)S(1)} fusion(bf16[4096,400]{0,1:T(8,128)(2,1)S(1)} %bitcast.41, f32[1024,200]{0,1:T(8,128)S(1)} %get-tuple-element.13, f32[1024,200]{0,1:T(8,128)S(1)} %get-tuple-element.12), kind=kOutput, calls=%fused_computation.7 | convolution fusion | flops 3378053120 | bytes 13303808 | tf_op jit(solution)/shard_map/dot_general | solution.py:62
  224.4 3.6 fusion.13
  228.1 3.6 copy.62
  231.7 5.5 all-to-all-start.4
  237.2 5.8 copy.58
  244.9 8.1 %fusion.7 = f32[1024,400]{0,1:T(8,128)S(1)} fusion(bf16[1024,4096]{1,0:T(8,128)(2,1)} %copy-done.11, bf16[4096,400]{0,1:T(8,128)(2,1)} %bitcast.40, bf16[1024,1,400]{0,2,1:T(8,128)(2,1)} %copy.58, f32[1024]{0:T(1024)S(1)} %divide_add_fusion), kind=kOutput, calls=%fused_computation.21 | convolution fusion | flops 3356672000 | bytes 14127104 | tf_op jit(solution)/shard_map/dot_general | solution.py:66
  256.8 4.5 copy.49
  261.4 6.2 reshape.234
  267.5 13.4 %scatter_custom_fusion.1 = f32[4096,400]{1,0:T(8,128)} fusion(s32[2048]{0:T(1024)S(1)} %bitcast.45, f32[2048,400]{1,0:T(8,128)} %reshape.234, f32[]{:T(128)} %constant.10.clone.1), kind=kCustom, calls=%fused_computation.11 | custom fusion | bytes 6554112 | tf_op jit(solution)/shard_map/scatter | solution.py:82
  280.9 29.8 %all-to-all-done.4 = f32[4,1024,400]{1,2,0:T(8,128)} async-done(((f32[4,1024,400]{1,2,0:T(8,128)}), f32[4,1024,400]{1,2,0:T(8,128)}, u32[]{:S(2)}, u32[]{:S(2)}) %all-to-all-start.4) | async-done | bytes 6553632 | tf_op jit(solution)/shard_map/all_to_all | solution.py:72
  310.7 9.9 %all-to-all-start.3 = ((f32[64,64,400]{2,1,0:T(8,128)}), f32[64,64,400]{2,1,0:T(8,128)}, u32[]{:S(2)}, u32[]{:S(2)}) async-start(f32[64,64,400]{2,1,0:T(8,128)} %bitcast.34), calls=%async_computation.3 | async-start | bytes 16777216 | tf_op jit(solution)/shard_map/all_to_all | solution.py:83
  322.8 8.9 %scatter_custom_fusion.3 = f32[1345,400]{1,0:T(8,128)} fusion(s32[1024]{0:T(1024)S(1)} %get-tuple-element.18, f32[1024,400]{1,0:T(8,128)} %copy.53, f32[]{:T(128)} %constant.10.clone.1), kind=kCustom, calls=%fused_computation.26 | custom fusion | flops 409600 | bytes 2152512 | tf_op jit(solution)/shard_map/scatter-add | solution.py:79
  331.8 241.4 %all-reduce.3.cloned.1.call-done = f32[1345,400]{1,0:T(8,128)} async-done(((f32[1345,400]{1,0:T(8,128)}), f32[1345,400]{1,0:T(8,128)}) %all-reduce.3.cloned.1.call-update) | async-done | bytes 2152016 | tf_op jit(solution)/shard_map/psum | solution.py:25
  574.6 75.1 %all-reduce.5.cloned.1.call-done = f32[1345,400]{1,0:T(8,128)} async-done(((f32[1345,400]{1,0:T(8,128)}), f32[1345,400]{1,0:T(8,128)}) %all-reduce.5.cloned.1.call-update) | async-done | bytes 2152016 | tf_op jit(solution)/shard_map/psum | solution.py:25
  649.7 3.3 copy.55
  652.9 4.9 reduce_sum.29
  659.7 30.0 %scatter_custom_fusion.2 = f32[2048,400]{1,0:T(8,128)} fusion(s32[4096]{0:T(1024)S(1)} %bitcast.47, f32[4096,400]{1,0:T(8,128)} %bitcast.14, f32[]{:T(128)} %constant.10.clone.1), kind=kCustom, calls=%fused_computation.16 | custom fusion | flops 1638400 | bytes 3277312 | tf_op jit(solution)/shard_map/scatter-add | solution.py:89
  689.7 3.4 add_dynamic-update-slice_fusion
  693.1 5.2 copy.54
  (67 shorter events, 31.7 us)
Async XLA Ops:
  10.8 23.2 %copy-start.5 = (bf16[2048,400]{0,1:T(8,128)(2,1)S(1)}, bf16[2048,400]{0,1:T(8,128)(2,1)}, u32[]{:S(2)}) copy-start(bf16[2048,400]{0,1:T(8,128)(2,1)} %param.6) | copy-start | bytes 4915204
  21.3 19.7 %all-to-all-start = ((s32[64,1,64]{2,1,0:T(1,128)}), s32[64,1,64]{2,1,0:T(1,128)S(1)}, u32[]{:S(2)}, u32[]{:S(2)}) async-start(s32[64,1,64]{2,1,0:T(1,128)} %all_to_all.20), calls=%async_computation | async-start | bytes 65536 | tf_op jit(solution)/shard_map/all_to_all | solution.py:50
  43.1 44.1 %all-to-all-start.2 = ((bf16[4,1024,400]{1,2,0:T(8,128)(2,1)}), bf16[4,1024,400]{1,2,0:T(8,128)(2,1)}, u32[]{:S(2)}, u32[]{:S(2)}) async-start(bf16[4,1024,400]{1,2,0:T(8,128)(2,1)} %broadcast_in_dim.18), calls=%async_computation.2 | async-start | bytes 6553600 | tf_op jit(solution)/shard_map/all_to_all | solution.py:12
  87.2 8.2 %copy-start.9 = (bf16[1345,400]{0,1:T(8,128)(2,1)S(1)}, bf16[1345,400]{0,1:T(8,128)(2,1)}, u32[]{:S(2)}) copy-start(bf16[1345,400]{0,1:T(8,128)(2,1)} %param.7) | copy-start | bytes 3228004
  87.2 9.1 %copy-start.10 = (s32[1024]{0:T(1024)S(1)}, s32[1024]{0:T(1024)}, u32[]{:S(2)}) copy-start(s32[1024]{0:T(1024)} %param.10) | copy-start | bytes 12292
  87.2 100.9 %all-to-all-start.1 = ((bf16[64,64,400]{2,1,0:T(8,128)(2,1)}), bf16[64,64,400]{2,1,0:T(8,128)(2,1)}, u32[]{:S(2)}, u32[]{:S(2)}) async-start(bf16[64,64,400]{2,1,0:T(8,128)(2,1)} %bitcast.36), calls=%async_computation.1 | async-start | bytes 8388608 | tf_op jit(solution)/shard_map/all_to_all | solution.py:51
  207.1 7.3 %copy-start = (f32[1024,400]{0,1:T(8,128)S(1)}, f32[1024,400]{0,1:T(8,128)}, u32[]{:S(2)}) copy-start(f32[1024,400]{0,1:T(8,128)} %convert_element_type.40) | copy-start | bytes 4915204
  214.4 2.5 copy-start.6
  214.7 9.7 %copy-start.1 = (f32[1024,200]{0,1:T(8,128)}, f32[1024,200]{0,1:T(8,128)S(1)}, u32[]{:S(2)}) copy-start(f32[1024,200]{0,1:T(8,128)S(1)} %get-tuple-element.12) | copy-start | bytes 2457604
  214.7 9.7 %copy-start.3 = (f32[1024,200]{0,1:T(8,128)}, f32[1024,200]{0,1:T(8,128)S(1)}, u32[]{:S(2)}) copy-start(f32[1024,200]{0,1:T(8,128)S(1)} %get-tuple-element.13) | copy-start | bytes 2457604
  224.4 3.7 copy-start.11
  231.7 79.0 %all-to-all-start.4 = ((f32[4,1024,400]{1,2,0:T(8,128)}), f32[4,1024,400]{1,2,0:T(8,128)}, u32[]{:S(2)}, u32[]{:S(2)}) async-start(f32[4,1024,400]{1,2,0:T(8,128)} %bitcast.35), calls=%async_computation.4 | async-start | bytes 13107200 | tf_op jit(solution)/shard_map/all_to_all | solution.py:72
  254.9 1.1 copy-start.2
  254.9 1.4 copy-start.4
  310.7 10.2 %copy-start.7 = (f32[1024,200]{0,1:T(8,128)S(1)}, f32[1024,200]{0,1:T(8,128)}, u32[]{:S(2)}) copy-start(f32[1024,200]{0,1:T(8,128)} %get-tuple-element.8) | copy-start | bytes 2457604
  310.7 10.2 %copy-start.8 = (f32[1024,200]{0,1:T(8,128)S(1)}, f32[1024,200]{0,1:T(8,128)}, u32[]{:S(2)}) copy-start(f32[1024,200]{0,1:T(8,128)} %get-tuple-element.9) | copy-start | bytes 2457604
  310.7 349.0 %all-to-all-start.3 = ((f32[64,64,400]{2,1,0:T(8,128)}), f32[64,64,400]{2,1,0:T(8,128)}, u32[]{:S(2)}, u32[]{:S(2)}) async-start(f32[64,64,400]{2,1,0:T(8,128)} %bitcast.34), calls=%async_computation.3 | async-start | bytes 16777216 | tf_op jit(solution)/shard_map/all_to_all | solution.py:83
  320.6 252.6 %all-reduce.3.cloned.1.call-start = ((), (), s32[]{:S(2)}) async-start(), calls=%async_computation.5 | async-start | bytes 5537792 | tf_op jit(solution)/shard_map/psum | solution.py:25
  331.8 317.9 %all-reduce.5.cloned.1.call-start = ((), (), s32[]{:S(2)}) async-start(), calls=%async_computation.6 | async-start | bytes 5537792 | tf_op jit(solution)/shard_map/psum | solution.py:25
Sparse Core Ops, SparseCore 0:
  331.9 241.2 all-reduce.2
  575.7 73.8 all-reduce.4
